TPU v7x, 128 devices: a whole 4x4x4 slice. The times are simulated.
128 devices in a mesh: seq: 16 (over x, z_lo, core), heads: 8 (over z_hi, y).
Axes of the slice: x: 4, y: 4, z: 4 (z_hi: 2, z_lo: 2; z = z_hi * 2 + z_lo), core: 2. Of those that a mesh axis runs over, the one named last changes fastest.
Arguments:
- tokens: bfloat16 [4096, 5120], P('seq', 'heads'), may hold values from -6 to 6
- order: int32 [4096], replicated, may hold values from 0 to 4095, each once
- lengths: int32 [12], replicated, may hold values from 1 to 1024, 4096 in all
- block_table: int32 [12, 2], replicated, may hold values from 0 to 31, as said below
- destination: int32 [32], replicated, may hold values from 0 to 31, each once
- w_query: bfloat16 [5120, 5120], P(None, 'heads'), may hold values from -0.078125 to 0.078125
- key_weight: bfloat16 [5120, 1024], P(None, 'heads'), may hold values from -0.078125 to 0.078125
- value_weight: bfloat16 [5120, 1024], P(None, 'heads'), may hold values from -0.078125 to 0.078125
- w_out: bfloat16 [5120, 5120], P('heads'), may hold values from -0.078125 to 0.078125
- key_value_cache: bfloat16 [4, 32, 512, 2, 1024], P(None, None, 'seq', None, 'heads'), may hold values from -600 to 600
Outputs:
- attn_out: bfloat16 [4096, 5120], P('seq', 'heads')
- decode_cache: bfloat16 [4, 32, 512, 2, 1024], P(None, 'seq', None, None, 'heads')
Inputs may be any that keep to these rules, and one draw needn't show every extreme that they name: `block_table`: each of the 12 requests names 2 blocks; no block is named twice.
All inputs are finite; a program needn't handle non-finite values.
Results may differ from a plain program's by a relative error of at most 0.015.
The roundings to bfloat16 on the way count: a program that leaves them out, or rounds other values in their place, can miss the bound.
Values may be sent and summed in bfloat16 or wider, within the bound.
No kernel may reach another device: no remote copies, remote signals or barrier semaphores. Data moves between devices by JAX's collectives and lax.ppermute only.
A program may use at most 128 MiB of HBM per device.

v0:
```python
import jax
import jax.numpy as jnp
from jax import lax
from jax.sharding import PartitionSpec as P

QUERY_HEADS = 40
KEY_VALUE_HEADS = 8
HEAD_SIZE = 128
BLOCK_POSITIONS = 512
CB = 2


theta = 1000000.0
epsilon = 1e-06


def apply_rotary(value_rows, place):
    half = value_rows.shape[-1] // 2
    freq = theta ** (-2.0 * jnp.arange(half, dtype=jnp.float32) / value_rows.shape[-1])
    angle = place[:, None, None] * freq
    cosine = jnp.cos(angle)
    sine_part = jnp.sin(angle)
    first = value_rows[..., :half]
    second = value_rows[..., half:]
    return jnp.concatenate(
        [first * cosine - second * sine_part, second * cosine + first * sine_part], axis=-1
    )


def request_place(order, lengths):
    ends = jnp.cumsum(lengths)
    starts = ends - lengths
    request = jnp.sum((order[:, None] >= ends[None, :]).astype(jnp.int32), axis=1)
    labels = jnp.arange(lengths.shape[0], dtype=jnp.int32)
    begin = jnp.sum(jnp.where(request[:, None] == labels[None, :], starts[None, :], 0), axis=1)
    return (request, order - begin)


def group_span(count, limit):
    span = min(count, limit)
    while count % span != 0:
        span -= 1
    return span


def attend(carry, query_rows, request, position, piece, key_request, key_position):
    count = piece.shape[0]
    span = group_span(count, 2048)
    steps = count // span
    pieces = piece.reshape(steps, span, piece.shape[1], piece.shape[2], piece.shape[3])
    requests = key_request.reshape(steps, span)
    positions = key_position.reshape(steps, span)
    scale = query_rows.shape[-1] ** (-0.5)

    def one_group(state, items):
        top, total, accum = state
        block, block_request, block_position = items
        scores = (
            jnp.einsum(
                "qgah,kgh->qgak", query_rows, block[:, 0], preferred_element_type=jnp.float32
            )
            * scale
        )
        allowed = (block_request[None, :] == request[:, None]) & (
            block_position[None, :] <= position[:, None]
        )
        wide_mask = allowed[:, None, None, :]
        row_max = jnp.max(jnp.where(wide_mask, scores, -1e30), axis=-1)
        new_top = jnp.maximum(top, row_max)
        expo = jnp.where(wide_mask, jnp.exp(scores - new_top[..., None]), 0.0)
        fade = jnp.exp(top - new_top)
        total = total * fade + jnp.sum(expo, axis=-1)
        weights = expo.astype(jnp.bfloat16)
        accum = accum * fade[..., None] + jnp.einsum(
            "qgak,kgh->qgah", weights, block[:, 1], preferred_element_type=jnp.float32
        )
        return ((new_top, total, accum), None)

    carry, unused = lax.scan(one_group, carry, (pieces, requests, positions))
    return carry


def on_device(
    tokens,
    order,
    lengths,
    block_table,
    destination,
    w_query,
    key_weight,
    value_weight,
    w_out,
    key_value_cache,
):
    full = lax.all_gather(tokens, "heads", axis=1, tiled=True)
    rows = full.shape[0]
    wide = full.astype(jnp.float32)
    normed = (wide * lax.rsqrt(jnp.mean(wide * wide, axis=1, keepdims=True) + epsilon)).astype(
        jnp.bfloat16
    )
    local_heads = key_weight.shape[1] // HEAD_SIZE
    head_group = QUERY_HEADS // KEY_VALUE_HEADS
    query_rows = jnp.dot(normed, w_query, preferred_element_type=jnp.float32)
    key_rows = jnp.dot(normed, key_weight, preferred_element_type=jnp.float32)
    value_rows = jnp.dot(normed, value_weight, preferred_element_type=jnp.float32)
    device = lax.axis_index("seq")
    my_order = lax.dynamic_slice_in_dim(order, device * rows, rows)
    request, position = request_place(my_order, lengths)
    rotary_angles = (position + CB * BLOCK_POSITIONS).astype(jnp.float32)
    query_rows = apply_rotary(
        query_rows.reshape(rows, local_heads * head_group, HEAD_SIZE), rotary_angles
    ).astype(jnp.bfloat16)
    query_rows = query_rows.reshape(rows, local_heads, head_group, HEAD_SIZE)
    key_rows = (
        apply_rotary(key_rows.reshape(rows, local_heads, HEAD_SIZE), rotary_angles)
        .astype(jnp.bfloat16)
        .reshape(rows, local_heads * HEAD_SIZE)
    )
    packed = jnp.stack([key_rows, value_rows.astype(jnp.bfloat16)], axis=1)
    initial = (
        jnp.full((rows, local_heads, head_group), -1e30, jnp.float32),
        jnp.zeros((rows, local_heads, head_group), jnp.float32),
        jnp.zeros((rows, local_heads, head_group, HEAD_SIZE), jnp.float32),
    )
    piece = lax.all_gather(packed, "seq", axis=0, tiled=True)
    count = piece.shape[0]
    key_request, key_position = request_place(order, lengths)
    state = attend(
        initial,
        query_rows,
        request,
        position,
        piece.reshape(count, 2, local_heads, HEAD_SIZE),
        key_request,
        key_position,
    )
    layer_zero = key_value_cache[0]
    labels = jnp.arange(layer_zero.shape[0], dtype=jnp.int32)
    hits = (block_table[:, :, None] == labels[None, None, :]).astype(jnp.int32)
    request_label = jnp.arange(block_table.shape[0], dtype=jnp.int32)[:, None, None] + 1
    owner = jnp.sum(hits * request_label, axis=(0, 1)) - 1
    piece = lax.all_gather(layer_zero, "seq", axis=1, tiled=True)
    blocks = piece.shape[0]
    count = piece.shape[1]
    key_request = jnp.repeat(owner, count)
    key_position = jnp.full((blocks * count,), -1, jnp.int32)
    flat = piece.reshape(blocks * count, 2, local_heads, HEAD_SIZE)
    state = attend(state, query_rows, request, position, flat, key_request, key_position)
    top, total, accum = state
    attn = (
        (accum / total[..., None])
        .astype(jnp.bfloat16)
        .reshape(rows, local_heads * head_group * HEAD_SIZE)
    )
    partial_value = jnp.dot(attn, w_out, preferred_element_type=jnp.float32)
    attn_out = lax.psum_scatter(
        partial_value.astype(jnp.bfloat16), "heads", scatter_dimension=1, tiled=True
    )
    slots = destination.shape[0]
    slot_labels = jnp.arange(slots, dtype=jnp.int32)
    inverse = jnp.sum(
        jnp.where(destination[None, :] == slot_labels[:, None], slot_labels[None, :], 0), axis=1
    )
    arranged = jnp.take(key_value_cache, inverse, axis=1)
    decode_cache = lax.all_to_all(arranged, "seq", split_axis=1, concat_axis=2, tiled=True)
    return (attn_out, decode_cache)


def solution(mesh):
    placed = (
        P("seq", "heads"),
        P(),
        P(),
        P(),
        P(),
        P(None, "heads"),
        P(None, "heads"),
        P(None, "heads"),
        P("heads", None),
        P(None, None, "seq", None, "heads"),
    )
    return jax.shard_map(
        on_device,
        mesh=mesh,
        in_specs=placed,
        out_specs=(P("seq", "heads"), P(None, "seq", None, None, "heads")),
        check_vma=False,
    )
```

profile of v0, /device:TPU:0, one launch (start us, length us, event | category | flops | bytes accessed | tf_op | source)
XLA Modules:
  0.0 349.6 jit_solution(2960406639354724734)
XLA Ops:
  11.2 60.3 %all-gather.5.cloned.1.call-done = bf16[256,5120]{1,0:T(8,128)(2,1)} async-done(((bf16[256,640]{1,0:T(8,128)(2,1)}), bf16[256,5120]{1,0:T(8,128)(2,1)}) %all-gather.5.cloned.1.call-update) | async-done | bytes 2621456 | tf_op jit(solution)/shard_map/all_gather | solution.py:95
  71.5 2.5 fusion.40
  74.1 2.9 convolution_bitcast_fusion
  81.4 6.4 %fusion.56 = f32[256,640]{0,1:T(8,128)S(1)} fusion(bf16[5120,640]{1,0:T(8,128)(2,1)} %param.19, bf16[256,5120]{1,0:T(8,128)(2,1)} %all-gather.5.cloned.1.call-done, f32[256]{0:T(256)S(1)} %add_rsqrt_fusion), kind=kOutput, calls=%fused_computation.105 | convolution fusion | flops 1681653760 | bytes 9831424 | tf_op jit(solution)/shard_map/dot_general | solution.py:103
  88.2 26.8 %all-gather.7.cloned.1.call-done = bf16[4096,2,128]{0,2,1:T(8,128)(2,1)} async-done(((bf16[256,2,128]{0,2,1:T(8,128)(2,1)}), bf16[4096,2,128]{0,2,1:T(8,128)(2,1)}) %all-gather.7.cloned.1.call-update) | async-done | bytes 2097168 | tf_op jit(solution)/shard_map/all_gather | solution.py:125
  115.0 3.3 reshape_reshape.7
  118.3 3.9 %copy.57 = bf16[2,2048,2,1,128]{4,1,2,3,0:T(8,128)(2,1)} copy(bf16[2,2048,2,1,128]{1,0,4,2,3:T(2,128)(2,1)S(1)} %reshape_reshape.7) | data formatting | bytes 4194304
  122.2 36.5 %while.30 = (s32[]{:T(128)}, f32[256,1,5]{0,2,1:T(8,128)S(1)}, f32[256,1,5]{0,2,1:T(8,128)S(1)}, f32[256,1,5,128]{0,3,2,1:T(8,128)}, s32[2,2048]{1,0:T(2,128)S(1...) while((s32[]{:T(128)}, f32[256,1,5]{0,2,1:T(8,128)S(1)}, ...), condition=%wide.region_9.10_spmd.clone, body=%wide.region_6.9_spmd.clone.sunk | while | flops 1373085184 | bytes 85663968 | solution.py:79
  125.0 5.7 %fusion.81 = (f32[256,5]{0,1:T(8,128)S(1)}, f32[2048,256,5]{1,0,2:T(8,128)}) fusion(pred[256,2048]{0,1:T(8,128)(4,1)S(1)} %compare_and_fusion.6, bf16[256,1,5,128]{3,0,2,1:T(8,128)(2,1)S(1)} %get-tuple-element.434, bf16[2048,2,1,128]{3,0,2,1:T(8,128)(2,1)S(1)} %dynamic-slice_bitcast_fusion.5), kind=kOutput, calls=%fused_computation.29.clone.1 | convolution fusion | flops 678951680 | bytes 11867136 | tf_op jit(solution)/shard_map/while/body/eval_jaxpr/qgah,kgh->qgak/dot_general | solution.py:59
  130.8 5.6 %fusion.84 = f32[256,1,5,128]{0,3,2,1:T(8,128)S(1)} fusion(f32[2048,256,5]{1,0,2:T(8,128)} %get-tuple-element.399, f32[256,5]{0,1:T(8,128)S(1)} %bitcast.223, pred[256,2048]{0,1:T(8,128)(4,1)S(1)} %compare_and_fusion.6, f32[256,1,5,128]{0,3,2,1:T(8,128)S(1)} %copy-done.4, bf16[2048,2,1,128]{3,0,2,1:T(8,128)(2,1)S(1)} %dynamic-slice_bitcast_fusion.5, ...), kind=kOutput, calls=%fused_computation.39.clone.1 | convolution fusion | flops 682065920 | bytes 12861441 | tf_op jit(solution)/shard_map/while/body/eval_jaxpr/qgak,kgh->qgah/dot_general | solution.py:74
  143.2 5.8 %fusion.81 = (f32[256,5]{0,1:T(8,128)S(1)}, f32[2048,256,5]{1,0,2:T(8,128)}) fusion(pred[256,2048]{0,1:T(8,128)(4,1)S(1)} %compare_and_fusion.6, bf16[256,1,5,128]{3,0,2,1:T(8,128)(2,1)S(1)} %get-tuple-element.434, bf16[2048,2,1,128]{3,0,2,1:T(8,128)(2,1)S(1)} %dynamic-slice_bitcast_fusion.5), kind=kOutput, calls=%fused_computation.29.clone.1 | convolution fusion | flops 678951680 | bytes 11867136 | tf_op jit(solution)/shard_map/while/body/eval_jaxpr/qgah,kgh->qgak/dot_general | solution.py:59
  149.0 5.6 %fusion.84 = f32[256,1,5,128]{0,3,2,1:T(8,128)S(1)} fusion(f32[2048,256,5]{1,0,2:T(8,128)} %get-tuple-element.399, f32[256,5]{0,1:T(8,128)S(1)} %bitcast.223, pred[256,2048]{0,1:T(8,128)(4,1)S(1)} %compare_and_fusion.6, f32[256,1,5,128]{0,3,2,1:T(8,128)S(1)} %copy-done.4, bf16[2048,2,1,128]{3,0,2,1:T(8,128)(2,1)S(1)} %dynamic-slice_bitcast_fusion.5, ...), kind=kOutput, calls=%fused_computation.39.clone.1 | convolution fusion | flops 682065920 | bytes 12861441 | tf_op jit(solution)/shard_map/while/body/eval_jaxpr/qgak,kgh->qgah/dot_general | solution.py:74
  158.7 10.1 %all-gather.9.cloned.1.call-done = bf16[1,32,512,2,128]{4,2,1,3,0:T(8,128)(2,1)} async-done(((bf16[1,32,32,2,128]{4,2,1,3,0:T(8,128)(2,1)}), bf16[1,32,512,2,128]{4,2,1,3,0:T(8,128)(2,1)}) %all-gather.9.cloned.1.call-update) | async-done | bytes 8388624 | tf_op jit(solution)/shard_map/all_gather | solution.py:142
  168.9 65.7 %while.29 = (s32[]{:T(128)}, f32[256,1,5]{0,2,1:T(8,128)S(1)}, f32[256,1,5]{0,2,1:T(8,128)S(1)}, f32[256,1,5,128]{0,3,2,1:T(8,128)}, s32[8,2048]{1,0:T(8,128)S(1...) while((s32[]{:T(128)}, f32[256,1,5]{0,2,1:T(8,128)S(1)}, ...), condition=%wide.region_14.15_spmd, body=%wide.region_11.14_spmd.sunk | while | flops 1372393472 | bytes 43696804 | solution.py:79
  172.6 2.3 fusion.79
  174.8 2.2 fusion.78
  180.8 2.3 fusion.79
  183.1 2.2 fusion.78
  189.0 2.3 fusion.79
  197.2 2.3 fusion.79
  199.5 2.2 fusion.78
  205.4 2.3 fusion.79
  213.7 2.3 fusion.79
  221.9 2.3 fusion.79
  224.2 2.2 fusion.78
  230.1 2.3 fusion.79
  235.8 6.6 %convolution_convert_fusion = bf16[256,5120]{1,0:T(8,128)(2,1)} fusion(bf16[256,640]{0,1:T(8,128)(2,1)S(1)} %bitcast.226, bf16[640,5120]{1,0:T(8,128)(2,1)} %param.22), kind=kOutput, calls=%fused_computation.57 | convolution fusion | flops 1679032320 | bytes 9502720 | tf_op jit(solution)/shard_map/dot_general | solution.py:155
  242.4 4.4 %copy.73 = bf16[256,5120]{0,1:T(8,128)(2,1)} copy(bf16[256,5120]{1,0:T(8,128)(2,1)} %convolution_convert_fusion) | data formatting | bytes 5242880
  246.9 7.3 %gather_fusion = bf16[32,4,32,2,128]{4,3,2,1,0:T(2,128)(2,1)S(1)} fusion(bf16[4,32,32,2,128]{4,3,2,1,0:T(2,128)(2,1)} %param.23, s32[1024]{0:T(1024)S(1)} %pad_clamp_fusion), kind=kCustom, calls=%fused_computation | custom fusion | bytes 4194432 | tf_op jit(solution)/shard_map/jit(_take)/gather | solution.py:164
  256.2 32.5 %all_to_all.18 = bf16[4,32,32,2,128]{4,3,2,0,1:T(2,128)(2,1)S(1)} all-to-all(bf16[4,32,32,2,128]{4,3,2,0,1:T(2,128)(2,1)S(1)} %fusion.42), channel_id=1, replica_groups=mesh['seq'=16,'heads'=8] {'seq'}, dimensions={1} | all-to-all | bytes 4194304 | tf_op jit(solution)/shard_map/all_to_all | solution.py:165
  288.7 3.3 copy.64
  292.0 49.2 %reduce-scatter.4.cloned.1.call-done = bf16[640,256]{1,0:T(8,128)(2,1)} async-done(((bf16[5120,256]{1,0:T(8,128)(2,1)}), bf16[640,256]{1,0:T(8,128)(2,1)}) %reduce-scatter.4.cloned.1.call-update) | async-done | bytes 327696
  (188 shorter events, 65.4 us)
Async XLA Ops:
  7.2 66.9 %copy-start = (bf16[5120,128]{1,0:T(8,128)(2,1)S(1)}, bf16[5120,128]{1,0:T(8,128)(2,1)}, u32[]{:S(2)}) copy-start(bf16[5120,128]{1,0:T(8,128)(2,1)} %param.20) | copy-start | bytes 3932164
  7.2 70.1 %copy-start.10 = (bf16[5120,128]{1,0:T(8,128)(2,1)S(1)}, bf16[5120,128]{1,0:T(8,128)(2,1)}, u32[]{:S(2)}) copy-start(bf16[5120,128]{1,0:T(8,128)(2,1)} %param.21) | copy-start | bytes 3932164
  7.2 64.3 %all-gather.5.cloned.1.call-start = ((), (), s32[]{:S(2)}) async-start(), calls=%async_computation.2 | async-start | bytes 2949120 | tf_op jit(solution)/shard_map/all_gather | solution.py:95
  7.9 107.1 %all-gather.7.cloned.1.call-start = ((), (), s32[]{:S(2)}) async-start(), calls=%async_computation.3 | async-start | bytes 2228224 | tf_op jit(solution)/shard_map/all_gather | solution.py:125
  71.5 5.8 %copy-start.3 = (bf16[256,5120]{1,0:T(8,128)(2,1)S(1)}, bf16[256,5120]{1,0:T(8,128)(2,1)}, u32[]{:S(2)}) copy-start(bf16[256,5120]{1,0:T(8,128)(2,1)} %all-gather.5.cloned.1.call-done) | copy-start | bytes 7864324
  74.0 5.2 %slice-start = ((bf16[4,32,32,2,128]{4,3,2,1,0:T(2,128)(2,1)}), bf16[1,32,32,2,128]{4,3,2,1,0:T(2,128)(2,1)S(1)}, s32[]{:S(2)}) async-start(bf16[4,32,32,2,128]{4,3,2,1,0:T(2,128)(2,1)} %param.23), calls=%async_computation.6 | async-start | bytes 1048576 | tf_op jit(solution)/shard_map/slice | solution.py:137
  74.0 6.3 %copy-start.8 = (s32[4096]{0:T(1024)S(1)}, s32[4096]{0:T(1024)}, u32[]{:S(2)}) copy-start(s32[4096]{0:T(1024)} %param.15) | copy-start | bytes 49156
  74.1 6.6 %copy-start.9 = (s32[12,2]{0,1:T(2,128)S(1)}, s32[12,2]{0,1:T(2,128)}, u32[]{:S(2)}) copy-start(s32[12,2]{0,1:T(2,128)} %param.17) | copy-start | bytes 292
  79.1 89.7 %all-gather.9.cloned.1.call-start = ((), (), s32[]{:S(2)}) async-start(), calls=%async_computation.4 | async-start | bytes 8912896 | tf_op jit(solution)/shard_map/all_gather | solution.py:142
  80.1 261.1 %reduce-scatter.4.cloned.1.call-start = ((), (), s32[]{:S(2)}) async-start(), calls=%async_computation.5 | async-start | bytes 2949120
  125.0 5.8 %copy-start.4 = (f32[256,1,5,128]{0,3,2,1:T(8,128)S(1)}, f32[256,1,5,128]{0,3,2,1:T(8,128)}, u32[]{:S(2)}) copy-start(f32[256,1,5,128]{0,3,2,1:T(8,128)} %get-tuple-element.416) | copy-start | bytes 1966084 | tf_op jit(solution)/shard_map/while
  130.8 7.4 %copy-start.2 = (f32[2048,256,5]{1,0,2:T(8,128)S(1)}, f32[2048,256,5]{1,0,2:T(8,128)}, u32[]{:S(2)}) copy-start(f32[2048,256,5]{1,0,2:T(8,128)} %get-tuple-element.399) | copy-start | bytes 31457284 | tf_op jit(solution)/shard_map/while
  138.2 2.2 copy-start.5
  143.2 5.8 %copy-start.4 = (f32[256,1,5,128]{0,3,2,1:T(8,128)S(1)}, f32[256,1,5,128]{0,3,2,1:T(8,128)}, u32[]{:S(2)}) copy-start(f32[256,1,5,128]{0,3,2,1:T(8,128)} %get-tuple-element.416) | copy-start | bytes 1966084 | tf_op jit(solution)/shard_map/while
  149.0 7.4 %copy-start.2 = (f32[2048,256,5]{1,0,2:T(8,128)S(1)}, f32[2048,256,5]{1,0,2:T(8,128)}, u32[]{:S(2)}) copy-start(f32[2048,256,5]{1,0,2:T(8,128)} %get-tuple-element.399) | copy-start | bytes 31457284 | tf_op jit(solution)/shard_map/while
  156.4 2.2 copy-start.5
  170.7 1.8 copy-start.6
  174.8 2.2 copy-start.7
  183.0 2.2 copy-start.7
  187.2 1.8 copy-start.6
  191.3 2.2 copy-start.7
  195.4 1.8 copy-start.6
  199.5 2.2 copy-start.7
  203.6 1.8 copy-start.6
  207.7 2.2 copy-start.7
  211.8 1.8 copy-start.6
  215.9 2.2 copy-start.7
  220.1 1.8 copy-start.6
  224.1 2.2 copy-start.7
  232.4 2.2 copy-start.7
  242.4 4.4 %copy-start.11 = (s32[32]{0:T(128)S(1)}, s32[32]{0:T(128)}, u32[]{:S(2)}) copy-start(s32[32]{0:T(128)} %param.18) | copy-start | bytes 388
  254.3 88.8 %copy-start.1 = (bf16[5120,128]{1,0:T(8,128)(2,1)S(1)}, bf16[5120,128]{1,0:T(8,128)(2,1)}, u32[]{:S(2)}) copy-start(bf16[5120,128]{1,0:T(8,128)(2,1)} %param.20) | copy-start | bytes 3932164
  (2 other events, 3.7 us)
Sparse Core Ops, SparseCore 0:
  10.3 61.1 all-gather.4
  79.2 35.6 all-gather.6
  116.6 52.1 all-gather.8
  246.9 94.2 reduce-scatter.3
where the time goes:
time: 350 us
  waiting for transfers between devices  147 us (42%)
  matrix products  72.2 us (21%)
  local copies, waits for them, and re-layouts  43.2 us (12%)
  other arithmetic  39.1 us (11%)
  blocking collectives  32.5 us (9%)
  between operations  14 us (4%)
    all_gather x1, waiting for transfers between devices, on_device(): full = lax.all_gather(tokens, 'heads', axis=1, tiled=True)  60.3 us
    unnamed x5, waiting for transfers between devices  49.9 us
    all_to_all x1, blocking collectives, on_device(): lax.all_to_all(arranged, 'seq', split_axis=1, concat_axis=2, tiled=True)  32.5 us
    dot_general x10, matrix products, one_group(): jnp.einsum('qgak,kgh->qgah', weights, block[:, 1], preferred_element_type...  29.3 us
    all_gather x1, waiting for transfers between devices, on_device(): piece = lax.all_gather(packed, 'seq', axis=0, tiled=True)  26.8 us
    dot_general x10, matrix products, one_group(): jnp.einsum('qgah,kgh->qgak', query_rows, block[:, 0], preferred_element_t...  25.9 us
    reduce_sum x10, other arithmetic, one_group(): total = total * fade + jnp.sum(expo, axis=-1)  21.9 us
    squeeze x10, local copies, waits for them, and re-layouts, attend(): carry, unused = lax.scan(one_group, carry, (pieces, requests, positions))  13 us
  transfers between devices with their start and end apart: 4, of which 4 were waited for; matrix products, arithmetic and copies ran while one was open for 18% of the time, Pallas kernels for 0%

commit v1 on v0

--- a/solution.py
+++ b/solution.py
@@ -80,6 +80,25 @@
     return carry
 
 
+def hand_over(arranged, device):
+    parts = lax.psum(1, "seq")
+    layers, slots = arranged.shape[0], arranged.shape[1]
+    width = slots // parts
+    chunks = arranged.reshape(layers, parts, width, *arranged.shape[2:])
+    received = []
+    for shift in range(parts):
+        target = lax.rem(device + shift, parts)
+        chunk = lax.dynamic_index_in_dim(chunks, target, 1, keepdims=False)
+        if shift > 0:
+            pairs = [(i, (i + shift) % parts) for i in range(parts)]
+            chunk = lax.ppermute(chunk, "seq", pairs)
+        received.append(chunk)
+    stacked = jnp.stack(received, axis=2)
+    sources = lax.rem(device - jnp.arange(parts, dtype=jnp.int32) + parts, parts)
+    placed = jnp.take(stacked, sources, axis=2)
+    return placed.reshape(layers, width, parts * arranged.shape[2], *arranged.shape[3:])
+
+
 def on_device(
     tokens,
     order,
@@ -135,13 +154,11 @@
         key_position,
     )
     layer_zero = key_value_cache[0]
-    labels = jnp.arange(layer_zero.shape[0], dtype=jnp.int32)
-    hits = (block_table[:, :, None] == labels[None, None, :]).astype(jnp.int32)
-    request_label = jnp.arange(block_table.shape[0], dtype=jnp.int32)[:, None, None] + 1
-    owner = jnp.sum(hits * request_label, axis=(0, 1)) - 1
-    piece = lax.all_gather(layer_zero, "seq", axis=1, tiled=True)
+    used = jnp.take(layer_zero, block_table.reshape(-1), axis=0)
+    piece = lax.all_gather(used, "seq", axis=1, tiled=True)
     blocks = piece.shape[0]
     count = piece.shape[1]
+    owner = jnp.arange(blocks, dtype=jnp.int32) // block_table.shape[1]
     key_request = jnp.repeat(owner, count)
     key_position = jnp.full((blocks * count,), -1, jnp.int32)
     flat = piece.reshape(blocks * count, 2, local_heads, HEAD_SIZE)
@@ -162,7 +179,7 @@
         jnp.where(destination[None, :] == slot_labels[:, None], slot_labels[None, :], 0), axis=1
     )
     arranged = jnp.take(key_value_cache, inverse, axis=1)
-    decode_cache = lax.all_to_all(arranged, "seq", split_axis=1, concat_axis=2, tiled=True)
+    decode_cache = hand_over(arranged, device)
     return (attn_out, decode_cache)
 
 

time: 350 us -> 330 us (0.943); the launches traced: 350 us -> 326 us
  blocking collectives: 32.5 us -> 0 us
  local copies, waits for them, and re-layouts: 43.2 us -> 67.6 us
  waiting for transfers between devices: 147 us -> 125 us
  starting transfers between devices: 0.34 us -> 19.7 us
  matrix products: 72.2 us -> 55.5 us
    all_to_all x1 -> x0, blocking collectives: 32.5 us -> none  [on_device(): lax.all_to_all(arranged, 'seq', split_axis=1, concat_axis=2, tiled=True)]
    ppermute x0 -> x15, starting transfers between devices: none -> 19.4 us  [hand_over(): chunk = lax.ppermute(chunk, 'seq', pairs)]
    unnamed x20 -> x48, local copies, waits for them, and re-layouts: 11.4 us -> 30.5 us
    unnamed x5, waiting for transfers between devices: 49.9 us -> 35.1 us
    dot_general x10 -> x8, matrix products: 29.3 us -> 17.9 us  [one_group(): jnp.einsum('qgak,kgh->qgah', weights, block[:, 1], preferred_element_type...]
    all_gather x1, waiting for transfers between devices: 10.1 us -> 0.01 us  [on_device(): piece = lax.all_gather(used, 'seq', axis=1, tiled=True)]
    all_gather x0 -> x1, local copies, waits for them, and re-layouts: none -> 6.22 us  [on_device(): piece = lax.all_gather(used, 'seq', axis=1, tiled=True)]
    ppermute x0 -> x15, waiting for transfers between devices: none -> 4.32 us  [hand_over(): chunk = lax.ppermute(chunk, 'seq', pairs)]
  transfers between devices with their start and end apart: 4 -> 19, of which waited for: 4 -> 6; matrix products, arithmetic and copies ran while one was open for 18% -> 27% of each run, Pallas kernels for 0% -> 0%
where the time goes in v1:
time: 330 us; the launch traced here: 326 us
  waiting for transfers between devices  125 us (38%)
  local copies, waits for them, and re-layouts  67.6 us (20%)
  matrix products  55.5 us (17%)
  other arithmetic  42.5 us (13%)
  starting transfers between devices  19.7 us (6%)
  between operations  14.7 us (4%)
    all_gather x1, waiting for transfers between devices, on_device(): full = lax.all_gather(tokens, 'heads', axis=1, tiled=True)  60.3 us
    unnamed x5, waiting for transfers between devices  35.1 us
    unnamed x48, local copies, waits for them, and re-layouts  30.5 us
    reduce_sum x8, other arithmetic, one_group(): total = total * fade + jnp.sum(expo, axis=-1)  26.1 us
    all_gather x1, waiting for transfers between devices, on_device(): piece = lax.all_gather(packed, 'seq', axis=0, tiled=True)  25.1 us
    dot_general x8, matrix products, one_group(): jnp.einsum('qgah,kgh->qgak', query_rows, block[:, 0], preferred_element_t...  22.3 us
    ppermute x15, starting transfers between devices, hand_over(): chunk = lax.ppermute(chunk, 'seq', pairs)  19.4 us
    dot_general x8, matrix products, one_group(): jnp.einsum('qgak,kgh->qgah', weights, block[:, 1], preferred_element_type...  17.9 us
  transfers between devices with their start and end apart: 19, of which 6 were waited for; matrix products, arithmetic and copies ran while one was open for 27% of the time, Pallas kernels for 0%

profile of v1, /device:TPU:0, one launch (start us, length us, event | category | flops | bytes accessed | tf_op | source)
XLA Modules:
  0.0 325.7 jit_solution(6499059143095368082)
XLA Ops:
  11.2 60.3 %all-gather.4.cloned.1.call-done = bf16[256,5120]{1,0:T(8,128)(2,1)} async-done(((bf16[256,640]{1,0:T(8,128)(2,1)}), bf16[256,5120]{1,0:T(8,128)(2,1)}) %all-gather.4.cloned.1.call-update) | async-done | bytes 2621456 | tf_op jit(solution)/shard_map/all_gather | solution.py:114
  71.5 2.5 fusion.40
  81.3 6.4 %fusion.59 = f32[256,640]{0,1:T(8,128)S(1)} fusion(bf16[5120,640]{1,0:T(8,128)(2,1)} %param.19, bf16[256,5120]{1,0:T(8,128)(2,1)} %all-gather.4.cloned.1.call-done, f32[256]{0:T(256)S(1)} %add_rsqrt_fusion), kind=kOutput, calls=%fused_computation.158 | convolution fusion | flops 1681653760 | bytes 9831424 | tf_op jit(solution)/shard_map/dot_general | solution.py:122
  88.1 25.1 %all-gather.6.cloned.1.call-done = bf16[4096,2,128]{0,2,1:T(8,128)(2,1)} async-done(((bf16[256,2,128]{0,2,1:T(8,128)(2,1)}), bf16[4096,2,128]{0,2,1:T(8,128)(2,1)}) %all-gather.6.cloned.1.call-update) | async-done | bytes 2097168 | tf_op jit(solution)/shard_map/all_gather | solution.py:144
  113.2 3.3 %reshape_reshape.7 = bf16[2,2048,2,1,128]{1,0,4,2,3:T(2,128)(2,1)S(1)} reshape(bf16[4096,2,128]{0,2,1:T(8,128)(2,1)} %all-gather.6.cloned.1.call-done) | data formatting | bytes 4194304 | tf_op jit(solution)/shard_map/reshape;reshape | solution.py:50
  116.5 3.9 %copy.75 = bf16[2,2048,2,1,128]{4,1,2,3,0:T(8,128)(2,1)} copy(bf16[2,2048,2,1,128]{1,0,4,2,3:T(2,128)(2,1)S(1)} %reshape_reshape.7) | data formatting | bytes 4194304
  120.4 37.9 %while.30 = (s32[]{:T(128)}, f32[256,1,5]{0,2,1:T(8,128)S(1)}, f32[256,1,5]{0,2,1:T(8,128)S(1)}, f32[256,1,5,128]{0,3,2,1:T(8,128)}, s32[2,2048]{1,0:T(2,128)S(1...) while((s32[]{:T(128)}, f32[256,1,5]{0,2,1:T(8,128)S(1)}, ...), condition=%wide.region_9.10_spmd.clone, body=%wide.region_6.9_spmd.clone.sunk | while | flops 1373085184 | bytes 85663968 | solution.py:79
  123.2 5.8 %fusion.84 = (f32[256,5]{0,1:T(8,128)S(1)}, f32[2048,256,5]{1,0,2:T(8,128)}) fusion(pred[256,2048]{0,1:T(8,128)(4,1)S(1)} %compare_and_fusion.8, bf16[256,1,5,128]{3,0,2,1:T(8,128)(2,1)S(1)} %get-tuple-element.474, bf16[2048,2,1,128]{3,0,2,1:T(8,128)(2,1)S(1)} %dynamic-slice_bitcast_fusion.20), kind=kOutput, calls=%fused_computation.31.clone.1 | convolution fusion | flops 678951680 | bytes 11867136 | tf_op jit(solution)/shard_map/while/body/eval_jaxpr/qgah,kgh->qgak/dot_general | solution.py:59
  129.0 6.5 %fusion.86 = f32[256,5]{0,1:T(8,128)S(1)} fusion(f32[2048,256,5]{1,0,2:T(8,128)} %get-tuple-element.439, f32[256,5]{0,1:T(8,128)S(1)} %bitcast.295, pred[256,2048]{0,1:T(8,128)(4,1)S(1)} %compare_and_fusion.8), kind=kLoop, calls=%fused_computation.35.clone.1 | loop fusion | flops 10484480 | bytes 11020288 | tf_op jit(solution)/shard_map/while/body/eval_jaxpr/reduce_sum | solution.py:72
  136.3 2.2 fusion.87
  142.2 5.8 %fusion.84 = (f32[256,5]{0,1:T(8,128)S(1)}, f32[2048,256,5]{1,0,2:T(8,128)}) fusion(pred[256,2048]{0,1:T(8,128)(4,1)S(1)} %compare_and_fusion.8, bf16[256,1,5,128]{3,0,2,1:T(8,128)(2,1)S(1)} %get-tuple-element.474, bf16[2048,2,1,128]{3,0,2,1:T(8,128)(2,1)S(1)} %dynamic-slice_bitcast_fusion.20), kind=kOutput, calls=%fused_computation.31.clone.1 | convolution fusion | flops 678951680 | bytes 11867136 | tf_op jit(solution)/shard_map/while/body/eval_jaxpr/qgah,kgh->qgak/dot_general | solution.py:59
  148.0 6.5 %fusion.86 = f32[256,5]{0,1:T(8,128)S(1)} fusion(f32[2048,256,5]{1,0,2:T(8,128)} %get-tuple-element.439, f32[256,5]{0,1:T(8,128)S(1)} %bitcast.295, pred[256,2048]{0,1:T(8,128)(4,1)S(1)} %compare_and_fusion.8), kind=kLoop, calls=%fused_computation.35.clone.1 | loop fusion | flops 10484480 | bytes 11020288 | tf_op jit(solution)/shard_map/while/body/eval_jaxpr/reduce_sum | solution.py:72
  158.3 6.2 %copy.80 = bf16[24,512,2,128]{3,1,0,2:T(8,128)(2,1)} copy(bf16[24,512,2,128]{3,1,2,0:T(8,128)(2,1)} %all-gather.8.cloned.1.call-done) | data formatting | bytes 12582912 | tf_op jit(solution)/shard_map/all_gather | solution.py:158
  164.6 49.3 %while.29 = (s32[]{:T(128)}, f32[256,1,5]{0,2,1:T(8,128)S(1)}, f32[256,1,5]{0,2,1:T(8,128)S(1)}, f32[256,1,5,128]{0,3,2,1:T(8,128)S(1)}, s32[6,2048]{1,0:T(8,128...) while((s32[]{:T(128)}, f32[256,1,5]{0,2,1:T(8,128)S(1)}, ...), condition=%wide.region_13.14_spmd, body=%wide.region_10.13_spmd.sunk | while | flops 1372393472 | bytes 38453876 | solution.py:79
  170.7 2.3 fusion.82
  178.9 2.3 fusion.82
  187.0 2.3 fusion.82
  195.2 2.3 fusion.82
  203.4 2.3 fusion.82
  211.6 2.3 fusion.82
  213.9 6.6 %convolution_convert_fusion = bf16[256,5120]{1,0:T(8,128)(2,1)} fusion(bf16[256,640]{0,1:T(8,128)(2,1)S(1)} %bitcast.298, bf16[640,5120]{1,0:T(8,128)(2,1)} %param.22), kind=kOutput, calls=%fused_computation.59 | convolution fusion | flops 1679032320 | bytes 9502720 | tf_op jit(solution)/shard_map/dot_general | solution.py:172
  220.5 4.4 %copy.94 = bf16[256,5120]{0,1:T(8,128)(2,1)} copy(bf16[256,5120]{1,0:T(8,128)(2,1)} %convolution_convert_fusion) | data formatting | bytes 5242880
  226.5 6.4 %gather_fusion.1 = bf16[32,4,32,2,128]{4,3,2,1,0:T(2,128)(2,1)} fusion(bf16[4,32,32,2,128]{4,3,2,1,0:T(2,128)(2,1)S(1)} %copy-done.3, s32[1024]{0:T(1024)S(1)} %pad_clamp_fusion.1), kind=kCustom, calls=%fused_computation.1 | custom fusion | bytes 4194432 | tf_op jit(solution)/shard_map/jit(_take)/gather | solution.py:181
  241.2 2.3 collective-permute-done
  245.4 2.9 collective-permute-start.6
  249.9 2.6 collective-permute-start.7
  255.9 2.3 collective-permute-start.9
  259.7 3.4 %collective-permute-start.10 = (bf16[4,2,32,2,128]{4,2,3,1,0:T(8,128)(2,1)S(1)}, bf16[4,2,32,2,128]{4,2,3,1,0:T(8,128)(2,1)S(1)}, u32[]{:S(2)}, u32[]{:S(2)}) collective-permute-start(bf16[4,2,32,2,128]{4,2,3,1,0:T(8,128)(2,1)S(1)} %get-tuple-element.288), channel_id=1, source_target_pairs={{0,88},{8,96},{16,104},{24,112},{32,120},{40,0},{48,8},{56,16},{64... | collective-permute-start | bytes 393224 | tf_op jit(solution)/shard_map/ppermute | solution.py:94
  266.7 2.7 collective-permute-start.14
  275.5 2.6 gather_fusion.2
  279.0 3.5 %copy.85 = bf16[4,2,512,2,128]{4,3,2,1,0:T(2,128)(2,1)} copy(bf16[4,2,512,2,128]{4,2,3,1,0:T(8,128)(2,1)S(1)} %bitcast_select_fusion.2) | data formatting | bytes 4194304
  282.5 34.4 %reduce-scatter.4.cloned.1.call-done = bf16[640,256]{1,0:T(8,128)(2,1)} async-done(((bf16[5120,256]{1,0:T(8,128)(2,1)}), bf16[640,256]{1,0:T(8,128)(2,1)}) %reduce-scatter.4.cloned.1.call-update) | async-done | bytes 327696
  (206 shorter events, 88.1 us)
Async XLA Ops:
  7.2 66.9 %copy-start = (bf16[5120,128]{1,0:T(8,128)(2,1)S(1)}, bf16[5120,128]{1,0:T(8,128)(2,1)}, u32[]{:S(2)}) copy-start(bf16[5120,128]{1,0:T(8,128)(2,1)} %param.20) | copy-start | bytes 3932164
  7.2 64.3 %all-gather.4.cloned.1.call-start = ((), (), s32[]{:S(2)}) async-start(), calls=%async_computation.1 | async-start | bytes 2949120 | tf_op jit(solution)/shard_map/all_gather | solution.py:114
  7.9 105.3 %all-gather.6.cloned.1.call-start = ((), (), s32[]{:S(2)}) async-start(), calls=%async_computation.2 | async-start | bytes 2228224 | tf_op jit(solution)/shard_map/all_gather | solution.py:144
  71.5 2.5 copy-start.4
  75.2 2.3 copy-start.10
  76.7 3.0 copy-start.8
  76.7 3.5 %copy-start.14 = (s32[32]{0:T(128)S(1)}, s32[32]{0:T(128)}, u32[]{:S(2)}) copy-start(s32[32]{0:T(128)} %param.18) | copy-start | bytes 388
  77.4 81.0 %all-gather.8.cloned.1.call-start = ((), (), s32[]{:S(2)}) async-start(), calls=%async_computation.3 | async-start | bytes 6684672 | tf_op jit(solution)/shard_map/all_gather | solution.py:158
  79.4 237.5 %reduce-scatter.4.cloned.1.call-start = ((), (), s32[]{:S(2)}) async-start(), calls=%async_computation.4 | async-start | bytes 2949120
  80.3 7.4 %copy-start.11 = (s32[32]{0:T(128)}, s32[32]{0:T(128)S(1)}, u32[]{:S(2)}) copy-start(s32[32]{0:T(128)S(1)} %select_reduce_fusion.1) | copy-start | bytes 388
  123.2 12.3 %copy-start.5 = (f32[256,1,5,128]{0,3,2,1:T(8,128)S(1)}, f32[256,1,5,128]{0,3,2,1:T(8,128)}, u32[]{:S(2)}) copy-start(f32[256,1,5,128]{0,3,2,1:T(8,128)} %get-tuple-element.456) | copy-start | bytes 1966084 | tf_op jit(solution)/shard_map/while
  129.0 7.3 %copy-start.2 = (f32[2048,256,5]{1,0,2:T(8,128)S(1)}, f32[2048,256,5]{1,0,2:T(8,128)}, u32[]{:S(2)}) copy-start(f32[2048,256,5]{1,0,2:T(8,128)} %get-tuple-element.439) | copy-start | bytes 31457284 | tf_op jit(solution)/shard_map/while
  142.2 12.3 %copy-start.5 = (f32[256,1,5,128]{0,3,2,1:T(8,128)S(1)}, f32[256,1,5,128]{0,3,2,1:T(8,128)}, u32[]{:S(2)}) copy-start(f32[256,1,5,128]{0,3,2,1:T(8,128)} %get-tuple-element.456) | copy-start | bytes 1966084 | tf_op jit(solution)/shard_map/while
  148.0 7.3 %copy-start.2 = (f32[2048,256,5]{1,0,2:T(8,128)S(1)}, f32[2048,256,5]{1,0,2:T(8,128)}, u32[]{:S(2)}) copy-start(f32[2048,256,5]{1,0,2:T(8,128)} %get-tuple-element.439) | copy-start | bytes 31457284 | tf_op jit(solution)/shard_map/while
  158.3 6.2 %copy-start.7 = (f32[256,1,5,128]{0,3,2,1:T(8,128)S(1)}, f32[256,1,5,128]{0,3,2,1:T(8,128)}, u32[]{:S(2)}) copy-start(f32[256,1,5,128]{0,3,2,1:T(8,128)} %get-tuple-element.480) | copy-start | bytes 1966084
  225.6 7.4 %copy-start.9 = (s32[16,2]{1,0:T(8,128)S(1)}, s32[16,2]{1,0:T(8,128)}, u32[]{:S(2)}) copy-start(s32[16,2]{1,0:T(8,128)} %reduce_sum.86) | copy-start | bytes 388
  236.2 7.3 %collective-permute-start = (bf16[4,2,32,2,128]{4,2,3,1,0:T(8,128)(2,1)}, bf16[4,2,32,2,128]{4,2,3,1,0:T(8,128)(2,1)}, u32[]{:S(2)}, u32[]{:S(2)}) collective-permute-start(bf16[4,2,32,2,128]{4,2,3,1,0:T(8,128)(2,1)} %get-tuple-element.298), channel_id=1, source_target_pairs={{0,8},{8,16},{16,24},{24,32},{32,40},{40,48},{48,56},{56,64},{64,7... | collective-permute-start | bytes 393224 | tf_op jit(solution)/shard_map/ppermute | solution.py:94
  236.6 8.8 %collective-permute-start.1 = (bf16[4,2,32,2,128]{4,2,3,1,0:T(8,128)(2,1)}, bf16[4,2,32,2,128]{4,2,3,1,0:T(8,128)(2,1)}, u32[]{:S(2)}, u32[]{:S(2)}) collective-permute-start(bf16[4,2,32,2,128]{4,2,3,1,0:T(8,128)(2,1)} %get-tuple-element.297), channel_id=1, source_target_pairs={{0,16},{8,24},{16,32},{24,40},{32,48},{40,56},{48,64},{56,72},{64,... | collective-permute-start | bytes 393224 | tf_op jit(solution)/shard_map/ppermute | solution.py:94
  237.5 12.3 %collective-permute-start.2 = (bf16[4,2,32,2,128]{4,2,3,1,0:T(8,128)(2,1)}, bf16[4,2,32,2,128]{4,2,3,1,0:T(8,128)(2,1)}, u32[]{:S(2)}, u32[]{:S(2)}) collective-permute-start(bf16[4,2,32,2,128]{4,2,3,1,0:T(8,128)(2,1)} %get-tuple-element.296), channel_id=1, source_target_pairs={{0,24},{8,32},{16,40},{24,48},{32,56},{40,64},{48,72},{56,80},{64,... | collective-permute-start | bytes 393224 | tf_op jit(solution)/shard_map/ppermute | solution.py:94
  239.0 15.1 %collective-permute-start.3 = (bf16[4,2,32,2,128]{4,2,3,1,0:T(8,128)(2,1)}, bf16[4,2,32,2,128]{4,2,3,1,0:T(8,128)(2,1)}, u32[]{:S(2)}, u32[]{:S(2)}) collective-permute-start(bf16[4,2,32,2,128]{4,2,3,1,0:T(8,128)(2,1)} %get-tuple-element.295), channel_id=1, source_target_pairs={{0,32},{8,40},{16,48},{24,56},{32,64},{40,72},{48,80},{56,88},{64,... | collective-permute-start | bytes 393224 | tf_op jit(solution)/shard_map/ppermute | solution.py:94
  240.3 15.5 %collective-permute-start.4 = (bf16[4,2,32,2,128]{4,2,3,1,0:T(8,128)(2,1)S(1)}, bf16[4,2,32,2,128]{4,2,3,1,0:T(8,128)(2,1)}, u32[]{:S(2)}, u32[]{:S(2)}) collective-permute-start(bf16[4,2,32,2,128]{4,2,3,1,0:T(8,128)(2,1)S(1)} %get-tuple-element.294), channel_id=1, source_target_pairs={{0,40},{8,48},{16,56},{24,64},{32,72},{40,80},{48,88},{56,96},{64,... | collective-permute-start | bytes 393224 | tf_op jit(solution)/shard_map/ppermute | solution.py:94
  243.5 16.2 %collective-permute-start.5 = (bf16[4,2,32,2,128]{4,2,3,1,0:T(8,128)(2,1)S(1)}, bf16[4,2,32,2,128]{4,2,3,1,0:T(8,128)(2,1)S(1)}, u32[]{:S(2)}, u32[]{:S(2)}) collective-permute-start(bf16[4,2,32,2,128]{4,2,3,1,0:T(8,128)(2,1)S(1)} %get-tuple-element.293), channel_id=1, source_target_pairs={{0,48},{8,56},{16,64},{24,72},{32,80},{40,88},{48,96},{56,104},{64... | collective-permute-start | bytes 393224 | tf_op jit(solution)/shard_map/ppermute | solution.py:94
  245.4 18.4 %collective-permute-start.6 = (bf16[4,2,32,2,128]{4,2,3,1,0:T(8,128)(2,1)S(1)}, bf16[4,2,32,2,128]{4,2,3,1,0:T(8,128)(2,1)S(1)}, u32[]{:S(2)}, u32[]{:S(2)}) collective-permute-start(bf16[4,2,32,2,128]{4,2,3,1,0:T(8,128)(2,1)S(1)} %get-tuple-element.292), channel_id=1, source_target_pairs={{0,56},{8,64},{16,72},{24,80},{32,88},{40,96},{48,104},{56,112},{6... | collective-permute-start | bytes 393224 | tf_op jit(solution)/shard_map/ppermute | solution.py:94
  249.9 15.4 %collective-permute-start.7 = (bf16[4,2,32,2,128]{4,2,3,1,0:T(8,128)(2,1)S(1)}, bf16[4,2,32,2,128]{4,2,3,1,0:T(8,128)(2,1)S(1)}, u32[]{:S(2)}, u32[]{:S(2)}) collective-permute-start(bf16[4,2,32,2,128]{4,2,3,1,0:T(8,128)(2,1)S(1)} %get-tuple-element.291), channel_id=1, source_target_pairs={{0,64},{8,72},{16,80},{24,88},{32,96},{40,104},{48,112},{56,120},{... | collective-permute-start | bytes 393224 | tf_op jit(solution)/shard_map/ppermute | solution.py:94
  254.1 11.9 %collective-permute-start.8 = (bf16[4,2,32,2,128]{4,2,3,1,0:T(8,128)(2,1)S(1)}, bf16[4,2,32,2,128]{4,2,3,1,0:T(8,128)(2,1)S(1)}, u32[]{:S(2)}, u32[]{:S(2)}) collective-permute-start(bf16[4,2,32,2,128]{4,2,3,1,0:T(8,128)(2,1)S(1)} %get-tuple-element.290), channel_id=1, source_target_pairs={{0,72},{8,80},{16,88},{24,96},{32,104},{40,112},{48,120},{56,0},{6... | collective-permute-start | bytes 393224 | tf_op jit(solution)/shard_map/ppermute | solution.py:94
  255.9 10.8 %collective-permute-start.9 = (bf16[4,2,32,2,128]{4,2,3,1,0:T(8,128)(2,1)S(1)}, bf16[4,2,32,2,128]{4,2,3,1,0:T(8,128)(2,1)S(1)}, u32[]{:S(2)}, u32[]{:S(2)}) collective-permute-start(bf16[4,2,32,2,128]{4,2,3,1,0:T(8,128)(2,1)S(1)} %get-tuple-element.289), channel_id=1, source_target_pairs={{0,80},{8,88},{16,96},{24,104},{32,112},{40,120},{48,0},{56,8},{64... | collective-permute-start | bytes 393224 | tf_op jit(solution)/shard_map/ppermute | solution.py:94
  259.7 10.4 %collective-permute-start.10 = (bf16[4,2,32,2,128]{4,2,3,1,0:T(8,128)(2,1)S(1)}, bf16[4,2,32,2,128]{4,2,3,1,0:T(8,128)(2,1)S(1)}, u32[]{:S(2)}, u32[]{:S(2)}) collective-permute-start(bf16[4,2,32,2,128]{4,2,3,1,0:T(8,128)(2,1)S(1)} %get-tuple-element.288), channel_id=1, source_target_pairs={{0,88},{8,96},{16,104},{24,112},{32,120},{40,0},{48,8},{56,16},{64... | collective-permute-start | bytes 393224 | tf_op jit(solution)/shard_map/ppermute | solution.py:94
  263.8 7.0 %collective-permute-start.11 = (bf16[4,2,32,2,128]{4,2,3,1,0:T(8,128)(2,1)S(1)}, bf16[4,2,32,2,128]{4,2,3,1,0:T(8,128)(2,1)S(1)}, u32[]{:S(2)}, u32[]{:S(2)}) collective-permute-start(bf16[4,2,32,2,128]{4,2,3,1,0:T(8,128)(2,1)S(1)} %get-tuple-element.287), channel_id=1, source_target_pairs={{0,96},{8,104},{16,112},{24,120},{32,0},{40,8},{48,16},{56,24},{64... | collective-permute-start | bytes 393224 | tf_op jit(solution)/shard_map/ppermute | solution.py:94
  265.2 6.2 %collective-permute-start.12 = (bf16[4,2,32,2,128]{4,2,3,1,0:T(8,128)(2,1)S(1)}, bf16[4,2,32,2,128]{4,2,3,1,0:T(8,128)(2,1)S(1)}, u32[]{:S(2)}, u32[]{:S(2)}) collective-permute-start(bf16[4,2,32,2,128]{4,2,3,1,0:T(8,128)(2,1)S(1)} %get-tuple-element.286), channel_id=1, source_target_pairs={{0,104},{8,112},{16,120},{24,0},{32,8},{40,16},{48,24},{56,32},{64... | collective-permute-start | bytes 393224 | tf_op jit(solution)/shard_map/ppermute | solution.py:94
  265.9 7.5 %collective-permute-start.13 = (bf16[4,2,32,2,128]{4,2,3,1,0:T(8,128)(2,1)S(1)}, bf16[4,2,32,2,128]{4,2,3,1,0:T(8,128)(2,1)S(1)}, u32[]{:S(2)}, u32[]{:S(2)}) collective-permute-start(bf16[4,2,32,2,128]{4,2,3,1,0:T(8,128)(2,1)S(1)} %get-tuple-element.285), channel_id=1, source_target_pairs={{0,112},{8,120},{16,0},{24,8},{32,16},{40,24},{48,32},{56,40},{64,... | collective-permute-start | bytes 393224 | tf_op jit(solution)/shard_map/ppermute | solution.py:94
  266.7 8.2 %collective-permute-start.14 = (bf16[4,2,32,2,128]{4,2,3,1,0:T(8,128)(2,1)S(1)}, bf16[4,2,32,2,128]{4,2,3,1,0:T(8,128)(2,1)S(1)}, u32[]{:S(2)}, u32[]{:S(2)}) collective-permute-start(bf16[4,2,32,2,128]{4,2,3,1,0:T(8,128)(2,1)S(1)} %get-tuple-element.284), channel_id=1, source_target_pairs={{0,120},{8,0},{16,8},{24,16},{32,24},{40,32},{48,40},{56,48},{64,5... | collective-permute-start | bytes 393224 | tf_op jit(solution)/shard_map/ppermute | solution.py:94
  278.5 40.2 %copy-start.1 = (bf16[5120,128]{1,0:T(8,128)(2,1)S(1)}, bf16[5120,128]{1,0:T(8,128)(2,1)}, u32[]{:S(2)}) copy-start(bf16[5120,128]{1,0:T(8,128)(2,1)} %param.20) | copy-start | bytes 3932164
  (6 other events, 7.6 us)
Sparse Core Ops, SparseCore 0:
  10.3 61.1 all-gather.3
  77.5 35.6 all-gather.5
  114.9 42.3 all-gather.7
  225.1 91.7 reduce-scatter.3

commit v2 on v1

--- a/solution.py
+++ b/solution.py
@@ -2,6 +2,9 @@
 import jax.numpy as jnp
 from jax import lax
 from jax.sharding import PartitionSpec as P
+import functools
+from jax.experimental import pallas as pl
+from jax.experimental.pallas import tpu as pltpu
 
 QUERY_HEADS = 40
 KEY_VALUE_HEADS = 8
@@ -36,48 +39,91 @@
     return (request, order - begin)
 
 
-def group_span(count, limit):
-    span = min(count, limit)
-    while count % span != 0:
-        span -= 1
-    return span
-
-
-def attend(carry, query_rows, request, position, piece, key_request, key_position):
-    count = piece.shape[0]
-    span = group_span(count, 2048)
-    steps = count // span
-    pieces = piece.reshape(steps, span, piece.shape[1], piece.shape[2], piece.shape[3])
-    requests = key_request.reshape(steps, span)
-    positions = key_position.reshape(steps, span)
-    scale = query_rows.shape[-1] ** (-0.5)
-
-    def one_group(state, items):
-        top, total, accum = state
-        block, block_request, block_position = items
-        scores = (
-            jnp.einsum(
-                "qgah,kgh->qgak", query_rows, block[:, 0], preferred_element_type=jnp.float32
-            )
-            * scale
-        )
-        allowed = (block_request[None, :] == request[:, None]) & (
-            block_position[None, :] <= position[:, None]
-        )
-        wide_mask = allowed[:, None, None, :]
-        row_max = jnp.max(jnp.where(wide_mask, scores, -1e30), axis=-1)
-        new_top = jnp.maximum(top, row_max)
-        expo = jnp.where(wide_mask, jnp.exp(scores - new_top[..., None]), 0.0)
+from jax.experimental import pallas as pl
+from jax.experimental.pallas import tpu as pltpu
+
+TILE = 32
+CHUNK = 256
+
+
+def _attn_body(tables, q_ref, o_ref, rs_ref, req_ref, kv_ref, cache_ref, out_ref, *, group, scale):
+    t = pl.program_id(0)
+    rows = q_ref.shape[1]
+    size = q_ref.shape[2]
+    q = q_ref[...].reshape(group * rows, size)
+    o_row = o_ref[...]
+    rs_row = rs_ref[...]
+    req_row = req_ref[...]
+
+    def update(carry, keys, values, mask):
+        top, total, accum = carry
+        width = keys.shape[0]
+        scores = lax.dot_general(q, keys, (((1,), (1,)), ((), ())), preferred_element_type=jnp.float32) * scale
+        scores = scores.reshape(group, rows, width)
+        scores = jnp.where(mask[None], scores, -1e30).reshape(group * rows, width)
+        new_top = jnp.maximum(top, jnp.max(scores, axis=1, keepdims=True))
+        expo = jnp.exp(scores - new_top).reshape(group, rows, width)
+        expo = jnp.where(mask[None], expo, 0.0).reshape(group * rows, width)
         fade = jnp.exp(top - new_top)
-        total = total * fade + jnp.sum(expo, axis=-1)
-        weights = expo.astype(jnp.bfloat16)
-        accum = accum * fade[..., None] + jnp.einsum(
-            "qgak,kgh->qgah", weights, block[:, 1], preferred_element_type=jnp.float32
-        )
-        return ((new_top, total, accum), None)
-
-    carry, unused = lax.scan(one_group, carry, (pieces, requests, positions))
-    return carry
+        total = total * fade + jnp.sum(expo, axis=1, keepdims=True)
+        accum = accum * fade + jnp.dot(expo.astype(jnp.bfloat16), values, preferred_element_type=jnp.float32)
+        return (new_top, total, accum)
+
+    def cached(r, carry):
+        mask = req_row == r
+        for j in range(2):
+            block = cache_ref[2 * r + j]
+            carry = update(carry, block[:, :size], block[:, size:], mask)
+        return carry
+
+    def fresh(c, carry):
+        start = pl.multiple_of(c * CHUNK, CHUNK)
+        block = kv_ref[pl.ds(start, CHUNK), :]
+        index = start + lax.broadcasted_iota(jnp.int32, (1, CHUNK), 1)
+        mask = (index >= rs_row) & (index <= o_row)
+        return update(carry, block[:, :size], block[:, size:], mask)
+
+    carry = (
+        jnp.full((group * rows, 1), -1e30, jnp.float32),
+        jnp.zeros((group * rows, 1), jnp.float32),
+        jnp.zeros((group * rows, size), jnp.float32),
+    )
+    carry = lax.fori_loop(tables[0, t], tables[1, t] + 1, cached, carry)
+    carry = lax.fori_loop(tables[2, t], tables[3, t] + 1, fresh, carry)
+    top, total, accum = carry
+    out_ref[...] = (accum / total).reshape(group, rows, size).astype(out_ref.dtype)
+
+
+def sparse_attention(q_sorted, o_sorted, rs_sorted, req_sorted, kv_sorted, cache, interpret=False):
+    group, count, size = q_sorted.shape
+    tiles = count // TILE
+    firsts = jnp.arange(tiles) * TILE
+    lasts = firsts + TILE - 1
+    tables = jnp.stack([
+        req_sorted[firsts], req_sorted[lasts], rs_sorted[firsts] // CHUNK, o_sorted[lasts] // CHUNK
+    ]).astype(jnp.int32)
+    col = lambda v: v.reshape(count, 1).astype(jnp.int32)
+    body = functools.partial(_attn_body, group=group, scale=size ** (-0.5))
+    spec = pltpu.PrefetchScalarGridSpec(
+        num_scalar_prefetch=1,
+        grid=(tiles,),
+        in_specs=[
+            pl.BlockSpec((group, TILE, size), lambda t, tb: (0, t, 0)),
+            pl.BlockSpec((TILE, 1), lambda t, tb: (t, 0)),
+            pl.BlockSpec((TILE, 1), lambda t, tb: (t, 0)),
+            pl.BlockSpec((TILE, 1), lambda t, tb: (t, 0)),
+            pl.BlockSpec(kv_sorted.shape, lambda t, tb: (0, 0)),
+            pl.BlockSpec(cache.shape, lambda t, tb: (0, 0, 0)),
+        ],
+        out_specs=pl.BlockSpec((group, TILE, size), lambda t, tb: (0, t, 0)),
+    )
+    return pl.pallas_call(
+        body,
+        grid_spec=spec,
+        out_shape=jax.ShapeDtypeStruct(q_sorted.shape, jnp.bfloat16),
+        compiler_params=pltpu.CompilerParams(dimension_semantics=("arbitrary",)),
+        interpret=interpret,
+    )(tables, q_sorted, col(o_sorted), col(rs_sorted), col(req_sorted), kv_sorted, cache)
 
 
 def hand_over(arranged, device):
@@ -135,40 +181,39 @@
         .astype(jnp.bfloat16)
         .reshape(rows, local_heads * HEAD_SIZE)
     )
-    packed = jnp.stack([key_rows, value_rows.astype(jnp.bfloat16)], axis=1)
-    initial = (
-        jnp.full((rows, local_heads, head_group), -1e30, jnp.float32),
-        jnp.zeros((rows, local_heads, head_group), jnp.float32),
-        jnp.zeros((rows, local_heads, head_group, HEAD_SIZE), jnp.float32),
-    )
-    piece = lax.all_gather(packed, "seq", axis=0, tiled=True)
-    count = piece.shape[0]
-    key_request, key_position = request_place(order, lengths)
-    state = attend(
-        initial,
-        query_rows,
-        request,
-        position,
-        piece.reshape(count, 2, local_heads, HEAD_SIZE),
-        key_request,
-        key_position,
-    )
+    fresh_rows = jnp.concatenate(
+        [
+            key_rows.reshape(rows, local_heads, HEAD_SIZE),
+            value_rows.astype(jnp.bfloat16).reshape(rows, local_heads, HEAD_SIZE),
+        ],
+        axis=2,
+    )
+    gathered = lax.all_gather(fresh_rows, "seq", axis=0, tiled=True)
+    kv_sorted = jnp.take(gathered, jnp.argsort(order), axis=0)
     layer_zero = key_value_cache[0]
     used = jnp.take(layer_zero, block_table.reshape(-1), axis=0)
-    piece = lax.all_gather(used, "seq", axis=1, tiled=True)
-    blocks = piece.shape[0]
-    count = piece.shape[1]
-    owner = jnp.arange(blocks, dtype=jnp.int32) // block_table.shape[1]
-    key_request = jnp.repeat(owner, count)
-    key_position = jnp.full((blocks * count,), -1, jnp.int32)
-    flat = piece.reshape(blocks * count, 2, local_heads, HEAD_SIZE)
-    state = attend(state, query_rows, request, position, flat, key_request, key_position)
-    top, total, accum = state
-    attn = (
-        (accum / total[..., None])
-        .astype(jnp.bfloat16)
-        .reshape(rows, local_heads * head_group * HEAD_SIZE)
-    )
+    pool, span = used.shape[0], used.shape[1]
+    used = used.reshape(pool, span, 2, local_heads, HEAD_SIZE).transpose(0, 1, 3, 2, 4)
+    used = used.reshape(pool, span, local_heads, 2 * HEAD_SIZE)
+    cache = lax.all_gather(used, "seq", axis=1, tiled=True)
+    perm = jnp.argsort(my_order)
+    o_sorted = jnp.take(my_order, perm)
+    rs_sorted = jnp.take(my_order - position, perm)
+    req_sorted = jnp.take(request, perm)
+    q_sorted = jnp.take(query_rows, perm, axis=0)
+    unsort = jnp.argsort(perm)
+    outs = []
+    for head in range(local_heads):
+        result = sparse_attention(
+            q_sorted[:, head].transpose(1, 0, 2),
+            o_sorted,
+            rs_sorted,
+            req_sorted,
+            kv_sorted[:, head],
+            cache[:, :, head],
+        )
+        outs.append(jnp.take(result, unsort, axis=1).transpose(1, 0, 2))
+    attn = jnp.stack(outs, axis=1).reshape(rows, local_heads * head_group * HEAD_SIZE)
     partial_value = jnp.dot(attn, w_out, preferred_element_type=jnp.float32)
     attn_out = lax.psum_scatter(
         partial_value.astype(jnp.bfloat16), "heads", scatter_dimension=1, tiled=True

time: 330 us -> 305 us (0.924); the launches traced: 326 us -> 306 us
  matrix products: 55.5 us -> 13.2 us
  Pallas kernels: 0 us -> 32.4 us
  other arithmetic: 42.5 us -> 27.2 us
  local copies, waits for them, and re-layouts: 67.6 us -> 74.6 us
  waiting for transfers between devices: 125 us -> 120 us
  starting transfers between devices: 19.7 us -> 24.2 us
    dot_general x16 -> x0, matrix products: 40.2 us -> none  [the longest x8 22.3 us: one_group(): jnp.einsum('qgah,kgh->qgak', query_rows, block[:, 0], preferred_element_t...]
    pallas_call x0 -> x1, Pallas kernels: none -> 32.4 us  [sparse_attention(): pl.pallas_call(body, grid_spec=spec, out_shape=jax.ShapeDtypeStruct(q_sor...]
    gather x0 -> x10, local copies, waits for them, and re-layouts: none -> 27.1 us  [the longest x1 17 us: on_device(): kv_sorted = jnp.take(gathered, jnp.argsort(order), axis=0)]
    reduce_sum x8 -> x0, other arithmetic: 26.1 us -> none  [one_group(): total = total * fade + jnp.sum(expo, axis=-1)]
    sort x0 -> x3, other arithmetic: none -> 12.1 us  [the longest x1 5.77 us: on_device(): kv_sorted = jnp.take(gathered, jnp.argsort(order), axis=0)]
    squeeze x8 -> x1, local copies, waits for them, and re-layouts: 10.5 us -> 1.48 us  [on_device(): layer_zero = key_value_cache[0]]
    and x8 -> x2, other arithmetic: 6.04 us -> 0.02 us  [the longest x1 0.01 us: on_device(): kv_sorted = jnp.take(gathered, jnp.argsort(order), axis=0)]
    unnamed x48 -> x39, local copies, waits for them, and re-layouts: 30.5 us -> 25 us
  transfers between devices with their start and end apart: 19 -> 19, of which waited for: 6 -> 7; matrix products, arithmetic and copies ran while one was open for 27% -> 31% of each run, Pallas kernels for 0% -> 0%
where the time goes in v2:
time: 305 us; the launch traced here: 306 us
  waiting for transfers between devices  120 us (39%)
  local copies, waits for them, and re-layouts  74.6 us (24%)
  Pallas kernels  32.4 us (11%)
  other arithmetic  27.2 us (9%)
  starting transfers between devices  24.2 us (8%)
  between operations  14.2 us (5%)
  matrix products  13.2 us (4%)
    all_gather x1, waiting for transfers between devices, on_device(): full = lax.all_gather(tokens, 'heads', axis=1, tiled=True)  60.3 us
    unnamed x5, waiting for transfers between devices  34.8 us
    pallas_call x1, Pallas kernels, sparse_attention(): pl.pallas_call(body, grid_spec=spec, out_shape=jax.ShapeDtypeStruct(q_sor...  32.4 us
    unnamed x39, local copies, waits for them, and re-layouts  25 us
    ppermute x15, starting transfers between devices, hand_over(): chunk = lax.ppermute(chunk, 'seq', pairs)  23.9 us
    all_gather x1, waiting for transfers between devices, on_device(): cache = lax.all_gather(used, 'seq', axis=1, tiled=True)  21.3 us
    gather x1, local copies, waits for them, and re-layouts, on_device(): kv_sorted = jnp.take(gathered, jnp.argsort(order), axis=0)  17 us
    gather x1, local copies, waits for them, and re-layouts, on_device(): arranged = jnp.take(key_value_cache, inverse, axis=1)  6.15 us
  transfers between devices with their start and end apart: 19, of which 7 were waited for; matrix products, arithmetic and copies ran while one was open for 31% of the time, Pallas kernels for 0%

profile of v2, /device:TPU:0, one launch (start us, length us, event | category | flops | bytes accessed | tf_op | source)
XLA Modules:
  0.0 305.9 jit_solution(6906089936314425252)
XLA Ops:
  11.2 60.3 %all-gather.4.cloned.1.call-done = bf16[256,5120]{1,0:T(8,128)(2,1)} async-done(((bf16[256,640]{1,0:T(8,128)(2,1)}), bf16[256,5120]{1,0:T(8,128)(2,1)}) %all-gather.4.cloned.1.call-update) | async-done | bytes 2621456 | tf_op jit(solution)/shard_map/all_gather | solution.py:160
  71.5 2.5 fusion
  81.9 3.2 %sort.48 = (s32[256]{0:T(256)}, s32[256]{0:T(256)S(1)}) sort(s32[256]{0:T(256)S(1)} %dynamic_slice.52, s32[256]{0:T(256)S(1)} %iota.47), dimensions={0}, to_apply=%region_0.0 | sort | flops 2048 | bytes 4096 | tf_op jit(solution)/shard_map/jit(argsort)/sort | solution.py:199
  85.1 1.9 gather_fusion.10
  87.1 1.9 gather_fusion.11
  89.0 1.9 gather_fusion.12
  96.0 5.8 %sort.50 = (s32[4096]{0:T(1024)}, s32[4096]{0:T(1024)S(1)}) sort(s32[4096]{0:T(1024)S(1)} %copy-done.5, s32[4096]{0:T(1024)S(1)} %iota.51), dimensions={0}, to_apply=%region_6.8 | sort | flops 49152 | bytes 65536 | tf_op jit(solution)/shard_map/jit(argsort)/sort | solution.py:192
  101.8 3.2 %sort.49 = (s32[256]{0:T(256)}, s32[256]{0:T(256)S(1)}) sort(s32[256]{0:T(256)S(1)} %get-tuple-element.6, s32[256]{0:T(256)S(1)} %iota.48), dimensions={0}, to_apply=%region_1.0 | sort | flops 2048 | bytes 4096 | tf_op jit(solution)/shard_map/jit(argsort)/sort | solution.py:204
  106.3 5.8 %fusion.24 = f32[256,640]{0,1:T(8,128)S(1)} fusion(bf16[5120,640]{1,0:T(8,128)(2,1)} %param.17, bf16[256,5120]{1,0:T(8,128)(2,1)S(1)} %copy-done.4, f32[256]{0:T(256)S(1)} %add_rsqrt_fusion), kind=kOutput, calls=%fused_computation.138 | convolution fusion | flops 1681653760 | bytes 9831424 | tf_op jit(solution)/shard_map/dot_general | solution.py:168
  115.7 3.3 %copy.65 = bf16[4096,256]{1,0:T(8,128)(2,1)S(1)} copy(bf16[4096,256]{0,1:T(8,128)(2,1)} %bitcast.136) | data formatting | bytes 4194304 | tf_op jit(solution)/shard_map/all_gather | solution.py:191
  119.0 17.0 %gather_fusion.5 = bf16[4096,256]{1,0:T(8,128)(2,1)} fusion(bf16[4096,256]{1,0:T(8,128)(2,1)S(1)} %copy.65, s32[4096]{0:T(1024)S(1)} %fusion.14), kind=kCustom, calls=%fused_computation.8 | custom fusion | bytes 4210688 | tf_op jit(solution)/shard_map/jit(_take)/gather | solution.py:192
  136.0 2.9 broadcast_select_fusion.kv_ref
  138.9 21.3 %all-gather.8.cloned.1.call-done = bf16[24,512,1,256]{3,1,0,2:T(8,128)(2,1)} async-done(((bf16[24,32,1,256]{3,1,0,2:T(8,128)(2,1)}), bf16[24,512,1,256]{3,1,0,2:T(8,128)(2,1)}) %all-gather.8.cloned.1.call-update) | async-done | bytes 6291472 | tf_op jit(solution)/shard_map/all_gather | solution.py:198
  160.3 32.4 %shard_map.113 = bf16[5,256,128]{2,1,0:T(8,128)(2,1)} custom-call(s32[4,8]{1,0:T(4,128)} %pad_add_fusion.tables, bf16[5,256,128]{2,1,0:T(8,128)(2,1)} %fusion.5.q_ref, s32[256,1]{1,0:T(8,128)} %copy.68.o_ref, s32[256,1]{1,0:T(8,128)} %copy.69.rs_ref, s32[256,1]{1,0:T(8,128)} %copy.70.req_ref, bf16[4096,256]{1,0:T(8,128)(2,1)} %broadcast_select_fusion.kv_ref, ...), custom_call_target="tpu_custom_call" | custom-call | tf_op jit(solution)/shard_map/pallas_call | solution.py:120
  195.0 5.1 %convolution_convert_fusion = bf16[256,5120]{1,0:T(8,128)(2,1)S(1)} fusion(bf16[256,640]{0,1:T(8,128)(2,1)S(1)} %bitcast.137, bf16[640,5120]{1,0:T(8,128)(2,1)} %param.20), kind=kOutput, calls=%fused_computation.15 | convolution fusion | flops 1679032320 | bytes 9502720 | tf_op jit(solution)/shard_map/dot_general | solution.py:217
  200.1 2.6 copy.78
  204.2 6.1 %gather_fusion.8 = bf16[32,4,32,2,128]{4,3,2,1,0:T(2,128)(2,1)} fusion(bf16[4,32,32,2,128]{4,3,2,1,0:T(2,128)(2,1)S(1)} %copy-done.2, s32[1024]{0:T(1024)S(1)} %get-tuple-element.44), kind=kCustom, calls=%fused_computation.11 | custom fusion | bytes 4194432 | tf_op jit(solution)/shard_map/jit(_take)/gather | solution.py:226
  210.4 1.9 copy_select_fusion
  214.3 1.7 collective-permute-start.2
  216.0 2.4 collective-permute-start.3
  219.5 1.7 collective-permute-done
  223.7 1.7 collective-permute-start.6
  226.9 2.1 collective-permute-start.7
  230.6 1.9 collective-permute-start.8
  234.1 2.1 collective-permute-start.9
  237.8 2.4 collective-permute-start.10
  240.9 2.6 collective-permute-start.11
  244.2 3.5 %collective-permute-start.12 = (bf16[4,2,32,2,128]{4,2,3,1,0:T(8,128)(2,1)S(1)}, bf16[4,2,32,2,128]{4,2,3,1,0:T(8,128)(2,1)S(1)}, u32[]{:S(2)}, u32[]{:S(2)}) collective-permute-start(bf16[4,2,32,2,128]{4,2,3,1,0:T(8,128)(2,1)S(1)} %get-tuple-element.21), channel_id=1, source_target_pairs={{0,104},{8,112},{16,120},{24,0},{32,8},{40,16},{48,24},{56,32},{64... | collective-permute-start | bytes 393224 | tf_op jit(solution)/shard_map/ppermute | solution.py:140
  256.5 2.5 gather_fusion.9
  260.0 3.5 %copy.76 = bf16[4,2,512,2,128]{4,3,2,1,0:T(2,128)(2,1)} copy(bf16[4,2,512,2,128]{4,2,3,1,0:T(8,128)(2,1)S(1)} %bitcast_select_fusion) | data formatting | bytes 4194304
  263.4 34.1 %reduce-scatter.4.cloned.1.call-done = bf16[640,256]{1,0:T(8,128)(2,1)} async-done(((bf16[5120,256]{1,0:T(8,128)(2,1)}), bf16[640,256]{1,0:T(8,128)(2,1)}) %reduce-scatter.4.cloned.1.call-update) | async-done | bytes 327696
  297.5 1.9 copy.79
  (134 shorter events, 48.4 us)
Async XLA Ops:
  7.2 66.9 %copy-start = (bf16[5120,128]{1,0:T(8,128)(2,1)S(1)}, bf16[5120,128]{1,0:T(8,128)(2,1)}, u32[]{:S(2)}) copy-start(bf16[5120,128]{1,0:T(8,128)(2,1)} %param.18) | copy-start | bytes 3932164
  7.2 64.3 %all-gather.4.cloned.1.call-start = ((), (), s32[]{:S(2)}) async-start(), calls=%async_computation.1 | async-start | bytes 2949120 | tf_op jit(solution)/shard_map/all_gather | solution.py:160
  7.9 107.8 %all-gather.6.cloned.1.call-start = ((), (), s32[]{:S(2)}) async-start(), calls=%async_computation.2 | async-start | bytes 2228224 | tf_op jit(solution)/shard_map/all_gather | solution.py:191
  71.5 2.5 copy-start.3
  74.0 1.5 copy-start.7
  75.5 1.9 copy-start.6
  77.4 82.9 %all-gather.8.cloned.1.call-start = ((), (), s32[]{:S(2)}) async-start(), calls=%async_computation.3 | async-start | bytes 6684672 | tf_op jit(solution)/shard_map/all_gather | solution.py:198
  81.7 215.8 %reduce-scatter.4.cloned.1.call-start = ((), (), s32[]{:S(2)}) async-start(), calls=%async_computation.4 | async-start | bytes 2949120
  87.1 9.0 %copy-start.5 = (s32[4096]{0:T(1024)S(1)}, s32[4096]{0:T(1024)}, u32[]{:S(2)}) copy-start(s32[4096]{0:T(1024)} %param.13) | copy-start | bytes 49156
  87.1 18.5 %copy-start.8 = (s32[32]{0:T(128)S(1)}, s32[32]{0:T(128)}, u32[]{:S(2)}) copy-start(s32[32]{0:T(128)} %param.16) | copy-start | bytes 388
  91.0 15.3 %copy-start.4 = (bf16[256,5120]{1,0:T(8,128)(2,1)S(1)}, bf16[256,5120]{1,0:T(8,128)(2,1)}, u32[]{:S(2)}) copy-start(bf16[256,5120]{1,0:T(8,128)(2,1)} %all-gather.4.cloned.1.call-done) | copy-start | bytes 7864324
  202.6 1.6 copy-start.2
  213.7 7.5 %collective-permute-start = (bf16[4,2,32,2,128]{4,2,3,1,0:T(8,128)(2,1)}, bf16[4,2,32,2,128]{4,2,3,1,0:T(8,128)(2,1)}, u32[]{:S(2)}, u32[]{:S(2)}) collective-permute-start(bf16[4,2,32,2,128]{4,2,3,1,0:T(8,128)(2,1)} %get-tuple-element.33), channel_id=1, source_target_pairs={{0,8},{8,16},{16,24},{24,32},{32,40},{40,48},{48,56},{56,64},{64,7... | collective-permute-start | bytes 393224 | tf_op jit(solution)/shard_map/ppermute | solution.py:140
  213.8 9.8 %collective-permute-start.1 = (bf16[4,2,32,2,128]{4,2,3,1,0:T(8,128)(2,1)}, bf16[4,2,32,2,128]{4,2,3,1,0:T(8,128)(2,1)}, u32[]{:S(2)}, u32[]{:S(2)}) collective-permute-start(bf16[4,2,32,2,128]{4,2,3,1,0:T(8,128)(2,1)} %get-tuple-element.32), channel_id=1, source_target_pairs={{0,16},{8,24},{16,32},{24,40},{32,48},{40,56},{48,64},{56,72},{64,... | collective-permute-start | bytes 393224 | tf_op jit(solution)/shard_map/ppermute | solution.py:140
  214.3 12.6 %collective-permute-start.2 = (bf16[4,2,32,2,128]{4,2,3,1,0:T(8,128)(2,1)}, bf16[4,2,32,2,128]{4,2,3,1,0:T(8,128)(2,1)}, u32[]{:S(2)}, u32[]{:S(2)}) collective-permute-start(bf16[4,2,32,2,128]{4,2,3,1,0:T(8,128)(2,1)} %get-tuple-element.31), channel_id=1, source_target_pairs={{0,24},{8,32},{16,40},{24,48},{32,56},{40,64},{48,72},{56,80},{64,... | collective-permute-start | bytes 393224 | tf_op jit(solution)/shard_map/ppermute | solution.py:140
  216.0 14.6 %collective-permute-start.3 = (bf16[4,2,32,2,128]{4,2,3,1,0:T(8,128)(2,1)}, bf16[4,2,32,2,128]{4,2,3,1,0:T(8,128)(2,1)}, u32[]{:S(2)}, u32[]{:S(2)}) collective-permute-start(bf16[4,2,32,2,128]{4,2,3,1,0:T(8,128)(2,1)} %get-tuple-element.30), channel_id=1, source_target_pairs={{0,32},{8,40},{16,48},{24,56},{32,64},{40,72},{48,80},{56,88},{64,... | collective-permute-start | bytes 393224 | tf_op jit(solution)/shard_map/ppermute | solution.py:140
  218.4 15.6 %collective-permute-start.4 = (bf16[4,2,32,2,128]{4,2,3,1,0:T(8,128)(2,1)S(1)}, bf16[4,2,32,2,128]{4,2,3,1,0:T(8,128)(2,1)}, u32[]{:S(2)}, u32[]{:S(2)}) collective-permute-start(bf16[4,2,32,2,128]{4,2,3,1,0:T(8,128)(2,1)S(1)} %get-tuple-element.29), channel_id=1, source_target_pairs={{0,40},{8,48},{16,56},{24,64},{32,72},{40,80},{48,88},{56,96},{64,... | collective-permute-start | bytes 393224 | tf_op jit(solution)/shard_map/ppermute | solution.py:140
  221.1 16.6 %collective-permute-start.5 = (bf16[4,2,32,2,128]{4,2,3,1,0:T(8,128)(2,1)S(1)}, bf16[4,2,32,2,128]{4,2,3,1,0:T(8,128)(2,1)S(1)}, u32[]{:S(2)}, u32[]{:S(2)}) collective-permute-start(bf16[4,2,32,2,128]{4,2,3,1,0:T(8,128)(2,1)S(1)} %get-tuple-element.28), channel_id=1, source_target_pairs={{0,48},{8,56},{16,64},{24,72},{32,80},{40,88},{48,96},{56,104},{64... | collective-permute-start | bytes 393224 | tf_op jit(solution)/shard_map/ppermute | solution.py:140
  223.7 17.2 %collective-permute-start.6 = (bf16[4,2,32,2,128]{4,2,3,1,0:T(8,128)(2,1)S(1)}, bf16[4,2,32,2,128]{4,2,3,1,0:T(8,128)(2,1)S(1)}, u32[]{:S(2)}, u32[]{:S(2)}) collective-permute-start(bf16[4,2,32,2,128]{4,2,3,1,0:T(8,128)(2,1)S(1)} %get-tuple-element.27), channel_id=1, source_target_pairs={{0,56},{8,64},{16,72},{24,80},{32,88},{40,96},{48,104},{56,112},{6... | collective-permute-start | bytes 393224 | tf_op jit(solution)/shard_map/ppermute | solution.py:140
  226.9 17.2 %collective-permute-start.7 = (bf16[4,2,32,2,128]{4,2,3,1,0:T(8,128)(2,1)S(1)}, bf16[4,2,32,2,128]{4,2,3,1,0:T(8,128)(2,1)S(1)}, u32[]{:S(2)}, u32[]{:S(2)}) collective-permute-start(bf16[4,2,32,2,128]{4,2,3,1,0:T(8,128)(2,1)S(1)} %get-tuple-element.26), channel_id=1, source_target_pairs={{0,64},{8,72},{16,80},{24,88},{32,96},{40,104},{48,112},{56,120},{... | collective-permute-start | bytes 393224 | tf_op jit(solution)/shard_map/ppermute | solution.py:140
  230.6 17.7 %collective-permute-start.8 = (bf16[4,2,32,2,128]{4,2,3,1,0:T(8,128)(2,1)S(1)}, bf16[4,2,32,2,128]{4,2,3,1,0:T(8,128)(2,1)S(1)}, u32[]{:S(2)}, u32[]{:S(2)}) collective-permute-start(bf16[4,2,32,2,128]{4,2,3,1,0:T(8,128)(2,1)S(1)} %get-tuple-element.25), channel_id=1, source_target_pairs={{0,72},{8,80},{16,88},{24,96},{32,104},{40,112},{48,120},{56,0},{6... | collective-permute-start | bytes 393224 | tf_op jit(solution)/shard_map/ppermute | solution.py:140
  234.1 16.1 %collective-permute-start.9 = (bf16[4,2,32,2,128]{4,2,3,1,0:T(8,128)(2,1)S(1)}, bf16[4,2,32,2,128]{4,2,3,1,0:T(8,128)(2,1)S(1)}, u32[]{:S(2)}, u32[]{:S(2)}) collective-permute-start(bf16[4,2,32,2,128]{4,2,3,1,0:T(8,128)(2,1)S(1)} %get-tuple-element.24), channel_id=1, source_target_pairs={{0,80},{8,88},{16,96},{24,104},{32,112},{40,120},{48,0},{56,8},{64... | collective-permute-start | bytes 393224 | tf_op jit(solution)/shard_map/ppermute | solution.py:140
  237.8 13.7 %collective-permute-start.10 = (bf16[4,2,32,2,128]{4,2,3,1,0:T(8,128)(2,1)S(1)}, bf16[4,2,32,2,128]{4,2,3,1,0:T(8,128)(2,1)S(1)}, u32[]{:S(2)}, u32[]{:S(2)}) collective-permute-start(bf16[4,2,32,2,128]{4,2,3,1,0:T(8,128)(2,1)S(1)} %get-tuple-element.23), channel_id=1, source_target_pairs={{0,88},{8,96},{16,104},{24,112},{32,120},{40,0},{48,8},{56,16},{64... | collective-permute-start | bytes 393224 | tf_op jit(solution)/shard_map/ppermute | solution.py:140
  240.9 11.3 %collective-permute-start.11 = (bf16[4,2,32,2,128]{4,2,3,1,0:T(8,128)(2,1)S(1)}, bf16[4,2,32,2,128]{4,2,3,1,0:T(8,128)(2,1)S(1)}, u32[]{:S(2)}, u32[]{:S(2)}) collective-permute-start(bf16[4,2,32,2,128]{4,2,3,1,0:T(8,128)(2,1)S(1)} %get-tuple-element.22), channel_id=1, source_target_pairs={{0,96},{8,104},{16,112},{24,120},{32,0},{40,8},{48,16},{56,24},{64... | collective-permute-start | bytes 393224 | tf_op jit(solution)/shard_map/ppermute | solution.py:140
  244.2 8.6 %collective-permute-start.12 = (bf16[4,2,32,2,128]{4,2,3,1,0:T(8,128)(2,1)S(1)}, bf16[4,2,32,2,128]{4,2,3,1,0:T(8,128)(2,1)S(1)}, u32[]{:S(2)}, u32[]{:S(2)}) collective-permute-start(bf16[4,2,32,2,128]{4,2,3,1,0:T(8,128)(2,1)S(1)} %get-tuple-element.21), channel_id=1, source_target_pairs={{0,104},{8,112},{16,120},{24,0},{32,8},{40,16},{48,24},{56,32},{64... | collective-permute-start | bytes 393224 | tf_op jit(solution)/shard_map/ppermute | solution.py:140
  248.3 6.0 %collective-permute-start.13 = (bf16[4,2,32,2,128]{4,2,3,1,0:T(8,128)(2,1)S(1)}, bf16[4,2,32,2,128]{4,2,3,1,0:T(8,128)(2,1)S(1)}, u32[]{:S(2)}, u32[]{:S(2)}) collective-permute-start(bf16[4,2,32,2,128]{4,2,3,1,0:T(8,128)(2,1)S(1)} %get-tuple-element.20), channel_id=1, source_target_pairs={{0,112},{8,120},{16,0},{24,8},{32,16},{40,24},{48,32},{56,40},{64,... | collective-permute-start | bytes 393224 | tf_op jit(solution)/shard_map/ppermute | solution.py:140
  250.2 5.6 %collective-permute-start.14 = (bf16[4,2,32,2,128]{4,2,3,1,0:T(8,128)(2,1)S(1)}, bf16[4,2,32,2,128]{4,2,3,1,0:T(8,128)(2,1)S(1)}, u32[]{:S(2)}, u32[]{:S(2)}) collective-permute-start(bf16[4,2,32,2,128]{4,2,3,1,0:T(8,128)(2,1)S(1)} %get-tuple-element.19), channel_id=1, source_target_pairs={{0,120},{8,0},{16,8},{24,16},{32,24},{40,32},{48,40},{56,48},{64,5... | collective-permute-start | bytes 393224 | tf_op jit(solution)/shard_map/ppermute | solution.py:140
  259.5 39.9 %copy-start.1 = (bf16[5120,128]{1,0:T(8,128)(2,1)S(1)}, bf16[5120,128]{1,0:T(8,128)(2,1)}, u32[]{:S(2)}) copy-start(bf16[5120,128]{1,0:T(8,128)(2,1)} %param.18) | copy-start | bytes 3932164
Sparse Core Ops, SparseCore 0:
  10.3 61.1 all-gather.3
  77.5 38.1 all-gather.5
  117.3 42.8 all-gather.7
  202.8 94.6 reduce-scatter.3
